TPU v7x, 32 devices: a whole 2x2x4 slice. The times are simulated.
32 devices in a mesh: fsdp: 8 (over y, x, core), dp: 4 (over z).
Axes of the slice: x: 2, y: 2, z: 4, core: 2. Of those that a mesh axis runs over, the one named last changes fastest.
Arguments:
- tokens: bfloat16 [131072, 1024], P(('fsdp', 'dp')), may hold values from -6 to 6
- cotangent: bfloat16 [131072, 1024], P(('fsdp', 'dp')), may hold values from -6 to 6
- lengths: int32 [256], P(('fsdp', 'dp')), may hold values from 8 to 2048, as said below
- selected: int32 [16384], P(('fsdp', 'dp')), may hold values from 0 to 4095, as said below
- attn_in: bfloat16 [1024, 3072], P('fsdp'), may hold values from -0.1875 to 0.1875
- attn_out: bfloat16 [1024, 1024], P('fsdp'), may hold values from -0.75 to 0.75
- mlp_in: bfloat16 [1024, 4096], P('fsdp'), may hold values from -0.1875 to 0.1875
- mlp_out: bfloat16 [4096, 1024], P('fsdp'), may hold values from -0.09375 to 0.09375
- norm_attn: bfloat16 [1024], P('fsdp'), may hold values from 0.5 to 1.5
- norm_mlp: bfloat16 [1024], P('fsdp'), may hold values from 0.5 to 1.5
- router: bfloat16 [1024], replicated, may hold values from -0.1875 to 0.1875
Outputs:
- output: bfloat16 [131072, 1024], P(('fsdp', 'dp'))
- grad_tokens: bfloat16 [131072, 1024], P(('fsdp', 'dp'))
- grad_attn_in: float32 [1024, 3072], P('fsdp')
- grad_attn_out: float32 [1024, 1024], P('fsdp')
- grad_mlp_in: float32 [1024, 4096], P('fsdp')
- grad_mlp_out: float32 [4096, 1024], P('fsdp')
- grad_norm_attn: float32 [1024], P('fsdp')
- grad_norm_mlp: float32 [1024], P('fsdp')
- grad_router: float32 [1024], replicated
Inputs may be any that keep to these rules, and one draw needn't show every extreme that they name: `lengths`: each aligned block of 8 entries (one device's sequences, in order) holds multiples of 8 that sum to 4096; exactly one of them equals 2048. `selected`: each aligned block of 512 entries lists distinct positions within its device's 4096 tokens in ascending order; a sequence of length L has exactly L / 8 of its positions listed.
All inputs are finite; a program needn't handle non-finite values.
Results may differ from a plain program's by a relative error of at most 0.014.
Values may be sent and summed in bfloat16 or wider, within the bound.
No kernel may reach another device: no remote copies, remote signals or barrier semaphores. Data moves between devices by JAX's collectives and lax.ppermute only.
A program may use at most 192 MiB of HBM per device.

v0:
```python
import numpy as np
import jax
import jax.numpy as jnp
from jax import lax
from jax.sharding import PartitionSpec as P

HEADS = 16
HEAD = 64
EPS = 1e-06
MASKED = -1e30


def rms_scale(values, gain_vec):
    return values * lax.rsqrt(jnp.mean(values * values, axis=-1, keepdims=True) + EPS) * gain_vec


def seq_mask(lengths, selected):
    seq_ends = jnp.cumsum(lengths)
    owner_seq = jnp.sum((selected[:, None] >= seq_ends[None, :]).astype(jnp.int32), axis=1)
    return (owner_seq[:, None] == owner_seq[None, :]) & (selected[None, :] <= selected[:, None])


def split_heads(matrix):
    return matrix.reshape(matrix.shape[0], HEADS, HEAD)


def masked_scores(query_heads, key_heads, allowed, score_scale):
    scores = (
        jnp.einsum("qhd,khd->hqk", query_heads, key_heads, preferred_element_type=jnp.float32)
        * score_scale
    )
    return jnp.where(allowed[None], scores, MASKED)


def plane_layout(mesh):
    devs = np.asarray(mesh.devices)
    if devs.ndim != 2 or devs.shape[0] != 8:
        return False
    try:
        for j in range(devs.shape[1]):
            for i in range(8):
                here = devs[i, j]
                mate = devs[i ^ 1, j]
                if (
                    tuple(mate.coords) != tuple(here.coords)
                    or mate.core_on_chip == here.core_on_chip
                ):
                    return False
                steps = []
                for bit in (2, 4):
                    other = devs[i ^ bit, j]
                    if other.core_on_chip != here.core_on_chip:
                        return False
                    diff = [abs(a - b) for a, b in zip(other.coords, here.coords)]
                    if sorted(diff) != [0] * (len(diff) - 1) + [1]:
                        return False
                    steps.append(diff.index(1))
                if steps[0] == steps[1]:
                    return False
    except AttributeError:
        return False
    return True


def swap_pairs(bit, size):
    return [(i, i ^ bit) for i in range(size)]


def plane_reduce(grad):
    rows, cols = grad.shape
    part = rows // 8
    half = part // 2
    me = lax.axis_index("fsdp")
    core = me % 2
    xi = me // 2 % 2
    yi = me // 4
    blocks = grad.reshape(4, 2, part, cols)
    keep = lax.dynamic_index_in_dim(blocks, core, axis=1, keepdims=False)
    send = lax.dynamic_index_in_dim(blocks, 1 - core, axis=1, keepdims=False)
    got = lax.ppermute(send.astype(jnp.bfloat16), "fsdp", swap_pairs(1, 8))
    chip = keep + got.astype(jnp.float32)

    def pick(y, x):
        return lax.dynamic_index_in_dim(chip, y * 2 + x, axis=0, keepdims=False)

    own = pick(yi, xi)
    to_x = pick(yi, 1 - xi)
    to_y = pick(1 - yi, xi)
    to_d = pick(1 - yi, 1 - xi)
    first_x = lax.ppermute(
        jnp.stack([to_x[:half], to_d[:half]]).astype(jnp.bfloat16), "fsdp", swap_pairs(2, 8)
    ).astype(jnp.float32)
    first_y = lax.ppermute(
        jnp.stack([to_y[half:], to_d[half:]]).astype(jnp.bfloat16), "fsdp", swap_pairs(4, 8)
    ).astype(jnp.float32)
    own_a = own[:half] + first_x[0]
    pass_a = to_y[:half] + first_x[1]
    own_b = own[half:] + first_y[0]
    pass_b = to_x[half:] + first_y[1]
    second_y = lax.ppermute(pass_a.astype(jnp.bfloat16), "fsdp", swap_pairs(4, 8)).astype(
        jnp.float32
    )
    second_x = lax.ppermute(pass_b.astype(jnp.bfloat16), "fsdp", swap_pairs(2, 8)).astype(
        jnp.float32
    )
    shard = jnp.concatenate([own_a + second_y, own_b + second_x], axis=0)
    return lax.psum(shard.astype(jnp.bfloat16), "dp").astype(jnp.float32)


def plain_reduce(grad):
    shard = lax.psum_scatter(grad.astype(jnp.bfloat16), "fsdp", scatter_dimension=0, tiled=True)
    return lax.psum(shard, "dp").astype(jnp.float32)


def make_per_device(reduce_grad):

    def per_device(
        tokens,
        cotangent,
        lengths,
        selected,
        attn_in,
        attn_out,
        mlp_in,
        mlp_out,
        norm_attn,
        norm_mlp,
        router,
    ):
        model_width = tokens.shape[1]
        row_count = selected.shape[0]
        score_scale = HEAD ** (-0.5)
        w_qkv, gain_attn = (
            lax.all_gather(attn_in, "fsdp", axis=0, tiled=True),
            lax.all_gather(norm_attn, "fsdp", axis=0, tiled=True),
        )
        w_out = lax.all_gather(attn_out, "fsdp", axis=0, tiled=True)
        w_in, gain_mlp = (
            lax.all_gather(mlp_in, "fsdp", axis=0, tiled=True),
            lax.all_gather(norm_mlp, "fsdp", axis=0, tiled=True),
        )
        w_down = lax.all_gather(mlp_out, "fsdp", axis=0, tiled=True)
        gain_one = gain_attn.astype(jnp.float32)
        gain_two = gain_mlp.astype(jnp.float32)
        positions = lax.broadcasted_iota(jnp.int32, (row_count, tokens.shape[0]), 1)
        select = (selected[:, None] == positions).astype(jnp.bfloat16)
        routed = jnp.dot(select, tokens, preferred_element_type=jnp.float32)
        routed_low = routed.astype(jnp.bfloat16)
        router_rate = jnp.dot(routed_low, router, preferred_element_type=jnp.float32)
        allowed = seq_mask(lengths, selected)
        normed_float, norm_pull = jax.vjp(rms_scale, routed, gain_one)
        normed = normed_float.astype(jnp.bfloat16)
        qkv = jnp.dot(normed, w_qkv, preferred_element_type=jnp.float32).astype(jnp.bfloat16)
        query_heads = split_heads(qkv[:, :model_width])
        key_heads = split_heads(qkv[:, model_width : 2 * model_width])
        value_heads = split_heads(qkv[:, 2 * model_width :])
        scores = masked_scores(query_heads, key_heads, allowed, score_scale)
        highest = jnp.max(scores, axis=-1, keepdims=True)
        exponent = jnp.exp(scores - highest)
        row_total = jnp.sum(exponent, axis=-1, keepdims=True)
        probabilities = (exponent / row_total).astype(jnp.bfloat16)
        log_total = highest + jnp.log(row_total)
        attn_mix = jnp.einsum(
            "hqk,khd->qhd", probabilities, value_heads, preferred_element_type=jnp.float32
        )
        attn_mix = attn_mix.reshape(row_count, model_width).astype(jnp.bfloat16)
        attended = jnp.dot(attn_mix, w_out, preferred_element_type=jnp.float32)
        middle = routed + attended
        normed_two_float, middle_pull = jax.vjp(rms_scale, middle, gain_two)
        normed_two = normed_two_float.astype(jnp.bfloat16)
        pre_gelu = jnp.dot(normed_two, w_in, preferred_element_type=jnp.float32)
        active_float, gelu_pull = jax.vjp(jax.nn.gelu, pre_gelu)
        active = active_float.astype(jnp.bfloat16)
        expanded = jnp.dot(active, w_down, preferred_element_type=jnp.float32)
        update = attended + expanded
        branch = (router_rate[:, None] * update).astype(jnp.bfloat16)
        output = (
            tokens.astype(jnp.float32)
            + jnp.einsum("kt,kd->td", select, branch, preferred_element_type=jnp.float32)
        ).astype(jnp.bfloat16)
        cot_rows = jnp.dot(select, cotangent, preferred_element_type=jnp.float32)
        grad_rate = jnp.sum(cot_rows * update, axis=-1)
        grad_update = cot_rows * router_rate[:, None]
        grad_expanded = grad_update.astype(jnp.bfloat16)
        grad_down = jnp.einsum(
            "kf,kd->fd", active, grad_expanded, preferred_element_type=jnp.float32
        )
        shard_down = reduce_grad(grad_down)
        grad_active = jnp.einsum(
            "kd,fd->kf", grad_expanded, w_down, preferred_element_type=jnp.float32
        )
        (grad_inner_float,) = gelu_pull(grad_active)
        grad_inner = grad_inner_float.astype(jnp.bfloat16)
        grad_up = jnp.einsum(
            "kd,kf->df", normed_two, grad_inner, preferred_element_type=jnp.float32
        )
        shard_up = reduce_grad(grad_up)
        grad_normed_two = jnp.einsum(
            "kf,df->kd", grad_inner, w_in, preferred_element_type=jnp.float32
        )
        grad_middle, grad_gain_two = middle_pull(grad_normed_two)
        grad_attended = (grad_update + grad_middle).astype(jnp.bfloat16)
        grad_proj = jnp.einsum(
            "ka,kd->ad", attn_mix, grad_attended, preferred_element_type=jnp.float32
        )
        shard_proj = reduce_grad(grad_proj)
        grad_mix = jnp.einsum(
            "kd,ad->ka", grad_attended, w_out, preferred_element_type=jnp.float32
        ).astype(jnp.bfloat16)
        grad_mix_heads = split_heads(grad_mix)
        scores_again = masked_scores(query_heads, key_heads, allowed, score_scale)
        prob_float = jnp.where(allowed[None], jnp.exp(scores_again - log_total), 0.0)
        grad_probs = jnp.einsum(
            "qhd,khd->hqk", grad_mix_heads, value_heads, preferred_element_type=jnp.float32
        )
        row_delta = jnp.sum(prob_float * grad_probs, axis=-1, keepdims=True)
        grad_scores = (prob_float * (grad_probs - row_delta)).astype(jnp.bfloat16)
        prob_low = prob_float.astype(jnp.bfloat16)
        grad_query = (
            jnp.einsum("hqk,khd->qhd", grad_scores, key_heads, preferred_element_type=jnp.float32)
            * score_scale
        )
        grad_key = (
            jnp.einsum("hqk,qhd->khd", grad_scores, query_heads, preferred_element_type=jnp.float32)
            * score_scale
        )
        grad_value = jnp.einsum(
            "hqk,qhd->khd", prob_low, grad_mix_heads, preferred_element_type=jnp.float32
        )
        grad_qkv = jnp.concatenate(
            [
                grad_query.reshape(row_count, model_width),
                grad_key.reshape(row_count, model_width),
                grad_value.reshape(row_count, model_width),
            ],
            axis=1,
        ).astype(jnp.bfloat16)
        grad_proj_in = jnp.einsum("kd,ke->de", normed, grad_qkv, preferred_element_type=jnp.float32)
        shard_qkv = reduce_grad(grad_proj_in)
        grad_normed = jnp.einsum("ke,de->kd", grad_qkv, w_qkv, preferred_element_type=jnp.float32)
        grad_routed_norm, grad_gain_one = norm_pull(grad_normed)
        grad_routed = (
            grad_routed_norm + grad_middle + grad_rate[:, None] * router.astype(jnp.float32)
        ).astype(jnp.bfloat16)
        grad_tokens = (
            cotangent.astype(jnp.float32)
            + jnp.einsum("kt,kd->td", select, grad_routed, preferred_element_type=jnp.float32)
        ).astype(jnp.bfloat16)
        router_local = jnp.dot(grad_rate, routed, precision=lax.Precision.HIGHEST)
        small = lax.psum(
            jnp.concatenate([grad_gain_one, grad_gain_two, router_local]), ("fsdp", "dp")
        )
        gain_part = grad_gain_one.shape[0] // lax.axis_size("fsdp")
        me = lax.axis_index("fsdp")
        shard_gain_one = lax.dynamic_slice_in_dim(small, me * gain_part, gain_part)
        shard_gain_two = lax.dynamic_slice_in_dim(
            small, grad_gain_one.shape[0] + me * gain_part, gain_part
        )
        grad_router = small[2 * grad_gain_one.shape[0] :]
        return (
            output,
            grad_tokens,
            shard_qkv,
            shard_proj,
            shard_up,
            shard_down,
            shard_gain_one,
            shard_gain_two,
            grad_router,
        )

    return per_device


def solution(mesh):
    placed = (
        P(("fsdp", "dp"), None),
        P(("fsdp", "dp"), None),
        P(("fsdp", "dp")),
        P(("fsdp", "dp")),
        P("fsdp", None),
        P("fsdp", None),
        P("fsdp", None),
        P("fsdp", None),
        P("fsdp"),
        P("fsdp"),
        P(),
    )
    reduce_grad = plane_reduce if plane_layout(mesh) else plain_reduce
    return jax.shard_map(
        make_per_device(reduce_grad),
        mesh=mesh,
        in_specs=placed,
        out_specs=(
            P(("fsdp", "dp"), None),
            P(("fsdp", "dp"), None),
            P("fsdp", None),
            P("fsdp", None),
            P("fsdp", None),
            P("fsdp", None),
            P("fsdp"),
            P("fsdp"),
            P(),
        ),
        check_vma=False,
    )
```

profile of v0, /device:TPU:0, one launch (start us, length us, event | category | flops | bytes accessed | tf_op | source)
XLA Modules:
  0.0 639.2 jit_solution(1268586833503978225)
XLA Ops:
  12.9 10.4 %all-gather = bf16[8,1,128]{2,1,0:T(2,128)(2,1)S(1)} all-gather(bf16[1,1,128]{2,1,0:T(2,128)(2,1)} %bitcast.194), channel_id=1, replica_groups=mesh['fsdp'=8,'dp'=4] {'fsdp'}, dimensions={0}, use_global_device_ids=true | all-gather | bytes 2304 | tf_op jit(solution)/shard_map/all_gather | solution.py:135
  23.3 8.8 %all-gather.1 = bf16[8,1,128]{2,1,0:T(2,128)(2,1)S(1)} all-gather(bf16[1,1,128]{2,1,0:T(2,128)(2,1)} %bitcast.195), channel_id=1, replica_groups=mesh['fsdp'=8,'dp'=4] {'fsdp'}, dimensions={0}, use_global_device_ids=true | all-gather | bytes 2304 | tf_op jit(solution)/shard_map/all_gather | solution.py:140
  32.9 7.8 %multiply_reduce_fusion.7 = (f32[512]{0:T(512)S(1)}, f32[512,1024]{1,0:T(8,128)S(1)}) fusion(bf16[4096,1024]{1,0:T(8,128)(2,1)} %param.11, s32[512]{0:T(512)} %param.14), kind=kOutput, calls=%fused_computation.64 | convolution fusion | flops 4298112512 | bytes 10489856 | tf_op jit(solution)/shard_map/dot_general | solution.py:147
  41.4 9.3 %fusion.12 = f32[512,1024]{1,0:T(8,128)} fusion(bf16[4096,1024]{1,0:T(8,128)(2,1)} %param.12, s32[512]{0:T(512)S(1)} %copy-done.15), kind=kOutput, calls=%fused_computation.28 | convolution fusion | flops 4297064448 | bytes 10487808 | tf_op jit(solution)/shard_map/dot_general | solution.py:181
  50.7 7.4 %all-gather.7.cloned.1.call-done = bf16[1024,3072]{1,0:T(8,128)(2,1)} async-done(((bf16[128,3072]{1,0:T(8,128)(2,1)}), bf16[1024,3072]{1,0:T(8,128)(2,1)}) %all-gather.7.cloned.1.call-update) | async-done | bytes 6291472 | tf_op jit(solution)/shard_map/all_gather | solution.py:134
  58.0 6.6 %convolution_convert_fusion = bf16[512,3072]{1,0:T(8,128)(2,1)S(1)} fusion(bf16[1024,3072]{1,0:T(8,128)(2,1)} %all-gather.7.cloned.1.call-done, f32[512,1024]{1,0:T(8,128)S(1)} %get-tuple-element.59, f32[1024]{0:T(1024)S(1)} %bitcast.180, f32[512]{0:T(512)S(1)} %fusion.84), kind=kOutput, calls=%fused_computation.34 | convolution fusion | flops 3224371200 | bytes 11540480 | tf_op jit(solution)/shard_map/dot_general | solution.py:153
  72.4 8.8 %fusion.1 = (f32[16,512]{1,0:T(8,128)S(1)}, f32[16,512,512]{1,2,0:T(8,128)}) fusion(pred[512,512]{0,1:T(8,128)(4,1)S(1)} %compare_and_fusion, bf16[512,16,64]{0,2,1:T(8,128)(2,1)} %bitcast.161, bf16[512,16,64]{0,2,1:T(8,128)(2,1)S(1)} %bitcast.159), kind=kOutput, calls=%fused_computation.11 | convolution fusion | flops 549445632 | bytes 19169280 | tf_op jit(solution)/shard_map/qhd,khd->hqk/dot_general | solution.py:29
  81.3 9.3 %fusion = f32[16,512]{1,0:T(8,128)S(1)} fusion(f32[16,512,512]{1,2,0:T(8,128)} %get-tuple-element.61, f32[16,512]{1,0:T(8,128)S(1)} %get-tuple-element.60, pred[512,512]{0,1:T(8,128)(4,1)S(1)} %compare_and_fusion), kind=kLoop, calls=%fused_computation.8 | loop fusion | flops 16769024 | bytes 17104896 | tf_op jit(solution)/shard_map/reduce_sum | solution.py:160
  90.6 9.5 %fusion.26 = bf16[16,64,512]{2,1,0:T(8,128)(2,1)} fusion(bf16[512,16,64]{0,2,1:T(8,128)(2,1)} %bitcast.175, f32[16,512,512]{1,2,0:T(8,128)} %get-tuple-element.61, f32[16,512]{1,0:T(8,128)S(1)} %fusion, f32[16,512]{1,0:T(8,128)S(1)} %get-tuple-element.60, pred[512,512]{0,1:T(8,128)(4,1)S(1)} %compare_and_fusion), kind=kOutput, calls=%fused_computation.68 | convolution fusion | flops 558366720 | bytes 19202048 | tf_op jit(solution)/shard_map/hqk,khd->qhd/dot_general | solution.py:163
  105.3 38.6 %all-gather.11.cloned.1.call-done = bf16[1024,4096]{1,0:T(8,128)(2,1)} async-done(((bf16[128,4096]{1,0:T(8,128)(2,1)}), bf16[1024,4096]{1,0:T(8,128)(2,1)}) %all-gather.11.cloned.1.call-update) | async-done | bytes 8388624 | tf_op jit(solution)/shard_map/all_gather | solution.py:139
  143.9 7.8 %fusion.96 = f32[512,4096]{1,0:T(8,128)S(1)} fusion(bf16[1024,4096]{1,0:T(8,128)(2,1)} %all-gather.11.cloned.1.call-done, f32[512,1024]{1,0:T(8,128)} %get-tuple-element.18, f32[1024]{0:T(1024)S(1)} %bitcast.184, f32[512]{0:T(512)S(1)} %fusion.85), kind=kOutput, calls=%fused_computation.181 | convolution fusion | flops 4296540160 | bytes 18880512 | tf_op jit(solution)/shard_map/dot_general | solution.py:171
  155.4 9.2 %fusion.93 = f32[4096,1024]{1,0:T(8,128)} fusion(f32[512,1024]{1,0:T(8,128)S(1)} %copy-done.40, f32[512]{0:T(512)S(1)} %bitcast.189, f32[512,4096]{1,0:T(8,128)S(1)} %fusion.96), kind=kOutput, calls=%fused_computation.178 | convolution fusion | flops 4314890240 | bytes 27265024 | tf_op jit(solution)/shard_map/kf,kd->fd/dot_general | solution.py:185
  164.7 35.3 %all-gather.13.cloned.1.call-done = bf16[4096,1024]{1,0:T(8,128)(2,1)} async-done(((bf16[512,1024]{1,0:T(8,128)(2,1)}), bf16[4096,1024]{1,0:T(8,128)(2,1)}) %all-gather.13.cloned.1.call-update) | async-done | bytes 8388624 | tf_op jit(solution)/shard_map/all_gather | solution.py:142
  199.9 13.3 %fusion.8 = bf16[512,4096]{1,0:T(8,128)(2,1)S(1)} fusion(f32[512,4096]{1,0:T(8,128)} %copy-done.39, bf16[4096,1024]{1,0:T(8,128)(2,1)} %all-gather.13.cloned.1.call-done, f32[512,1024]{1,0:T(8,128)} %fusion.12, f32[512]{0:T(512)S(1)} %bitcast.190), kind=kOutput, calls=%fused_computation.18 | convolution fusion | flops 4337958912 | bytes 23070720 | tf_op jit(solution)/shard_map/kd,fd->kf/dot_general | solution.py:189
  215.3 8.4 %fusion.95 = f32[1024,4096]{1,0:T(8,128)} fusion(bf16[512,4096]{1,0:T(8,128)(2,1)S(1)} %fusion.8, f32[512,1024]{1,0:T(8,128)S(1)} %copy-done.4, f32[1024]{0:T(1024)S(1)} %bitcast.185, f32[512]{0:T(512)S(1)} %fusion.85), kind=kOutput, calls=%fused_computation.180 | convolution fusion | flops 4296540160 | bytes 23074816 | tf_op jit(solution)/shard_map/kd,kf->df/dot_general | solution.py:194
  223.7 11.5 %multiply_reduce_fusion.1 = (f32[1024]{0:T(1024)}, f32[512]{0:T(512)S(1)}, f32[512,1024]{1,0:T(8,128)}) fusion(f32[512,1024]{1,0:T(8,128)S(1)} %copy-done.4, f32[512]{0:T(512)S(1)} %fusion.85, f32[1024]{0:T(1024)S(1)} %bitcast.186, bf16[512,4096]{1,0:T(8,128)(2,1)} %copy-done.38, bf16[1024,4096]{1,0:T(8,128)(2,1)} %all-gather.11.cloned.1.call-done), kind=kOutput, calls=%fused_computation.49 | convolution fusion | flops 4298111488 | bytes 16789504 | tf_op jit(solution)/shard_map/kf,df->kd/dot_general | solution.py:198
  235.3 10.3 %multiply_reduce_fusion.3 = (f32[512]{0:T(512)S(1)}, bf16[512,1024]{1,0:T(8,128)(2,1)S(1)}, f32[512,1024]{1,0:T(8,128)}) fusion(f32[512,1024]{1,0:T(8,128)S(1)} %copy-done.41, f32[512,1024]{1,0:T(8,128)S(1)} %copy-done.4, f32[512]{0:T(512)S(1)} %multiply_multiply_fusion.3, f32[512]{0:T(512)S(1)} %fusion.85, f32[512,1024]{1,0:T(8,128)} %get-tuple-element.63, ...), kind=kOutput, calls=%fused_computation.54 | convolution fusion | flops 4319608320 | bytes 28323840 | tf_op jit(solution)/shard_map/dot_general | solution.py:174
  251.2 11.5 %fusion.27 = bf16[16,64,512]{2,1,0:T(8,128)(2,1)} fusion(bf16[512,16,64]{0,2,1:T(8,128)(2,1)} %bitcast.177, f32[16,512]{1,0:T(8,128)S(1)} %log_add_fusion, f32[16,512,512]{1,2,0:T(8,128)} %get-tuple-element.61, pred[512,512]{0,1:T(8,128)(4,1)S(1)} %compare_and_fusion), kind=kOutput, calls=%fused_computation.70 | convolution fusion | flops 558366720 | bytes 19169280 | tf_op jit(solution)/shard_map/hqk,qhd->khd/dot_general | solution.py:227
  262.8 12.5 %multiply_reduce_fusion = (f32[16,512]{1,0:T(8,128)S(1)}, f32[16,512,512]{1,2,0:T(8,128)}) fusion(f32[16,512]{1,0:T(8,128)S(1)} %log_add_fusion, f32[16,512,512]{1,2,0:T(8,128)} %get-tuple-element.61, pred[512,512]{0,1:T(8,128)(4,1)S(1)} %compare_and_fusion, bf16[512,16,64]{0,2,1:T(8,128)(2,1)S(1)} %bitcast.178, bf16[512,16,64]{0,2,1:T(8,128)(2,1)S(1)} %bitcast.176), kind=kOutput, calls=%fused_computation.2 | convolution fusion | flops 562028544 | bytes 35979264 | tf_op jit(solution)/shard_map/qhd,khd->hqk/dot_general | solution.py:213
  275.2 12.6 %multiply_convert_fusion = bf16[16,512,512]{1,2,0:T(8,128)(2,1)S(1)} fusion(f32[16,512,512]{1,2,0:T(8,128)} %get-tuple-element.66, f32[16,512]{1,0:T(8,128)S(1)} %get-tuple-element.65, f32[16,512]{1,0:T(8,128)S(1)} %log_add_fusion, f32[16,512,512]{1,2,0:T(8,128)} %get-tuple-element.61, pred[512,512]{0,1:T(8,128)(4,1)S(1)} %compare_and_fusion), kind=kLoop, calls=%fused_computation.1 | loop fusion | flops 29360128 | bytes 42270720 | tf_op jit(solution)/shard_map/convert_element_type | solution.py:217
  293.8 6.0 fusion.17
  307.4 6.0 fusion.16
  313.7 9.0 %multiply_reduce_fusion.2 = (f32[1024]{0:T(1024)}, f32[512]{0:T(512)S(1)}, f32[512,1024]{1,0:T(8,128)}) fusion(f32[512,1024]{1,0:T(8,128)S(1)} %get-tuple-element.59, f32[512]{0:T(512)S(1)} %copy-done.34, f32[1024]{0:T(1024)S(1)} %bitcast.182, bf16[1024,3072]{1,0:T(8,128)(2,1)} %all-gather.7.cloned.1.call-done, bf16[512,1024]{0,1:T(8,128)(2,1)} %bitcast.201, ...), kind=kOutput, calls=%fused_computation.50 | convolution fusion | flops 3233806848 | bytes 13643776 | tf_op jit(solution)/shard_map/ke,de->kd/dot_general | solution.py:240
  346.4 52.0 %psum.39 = f32[3072]{0:T(1024)} all-reduce(f32[3072]{0:T(1024)S(1)} %pad_maximum_fusion.15), channel_id=1, replica_groups=mesh['fsdp'=8,'dp'=4] {'fsdp','dp'}, use_global_device_ids=true, to_apply=%region_16.17 | all-reduce | flops 3072 | bytes 24576 | tf_op jit(solution)/shard_map/psum | solution.py:250
  419.7 10.3 %bitcast_add_fusion = f32[4,512,1024]{2,1,0:T(8,128)} fusion(bf16[4,512,1024]{2,1,0:T(8,128)(2,1)} %collective-permute-done.15, f32[4,2,512,1024]{3,2,1,0:T(8,128)} %bitcast.164, s32[]{:T(128)S(6)} %select_n.97), kind=kLoop, calls=%fused_computation.21 | loop fusion | flops 4194304 | bytes 20971524 | tf_op jit(solution)/shard_map/add | solution.py:81
  440.2 19.6 %collective-permute-done.18 = bf16[2,256,1024]{2,1,0:T(8,128)(2,1)S(1)} collective-permute-done((bf16[2,256,1024]{2,1,0:T(8,128)(2,1)S(1)}, bf16[2,256,1024]{2,1,0:T(8,128)(2,1)S(1)}, u32[]{:S(2)}, u32[]{:S(2)}) %collective-permute-start.18) | collective-permute-done | bytes 1048608 | tf_op jit(solution)/shard_map/ppermute | solution.py:93
  463.5 18.8 %collective-permute-done.13 = bf16[2,64,4096]{2,1,0:T(8,128)(2,1)S(1)} collective-permute-done((bf16[2,64,4096]{2,1,0:T(8,128)(2,1)S(1)}, bf16[2,64,4096]{2,1,0:T(8,128)(2,1)S(1)}, u32[]{:S(2)}, u32[]{:S(2)}) %collective-permute-start.13) | collective-permute-done | bytes 1048608 | tf_op jit(solution)/shard_map/ppermute | solution.py:93
  486.8 6.7 %collective-permute-done.17 = bf16[256,1024]{1,0:T(8,128)(2,1)S(1)} collective-permute-done((bf16[256,1024]{1,0:T(8,128)(2,1)S(1)}, bf16[256,1024]{1,0:T(8,128)(2,1)S(1)}, u32[]{:S(2)}, u32[]{:S(2)}) %collective-permute-start.17) | collective-permute-done | bytes 524320 | tf_op jit(solution)/shard_map/ppermute | solution.py:100
  495.8 5.9 collective-permute-done.12
  504.3 10.0 %add_convert_fusion.1 = bf16[4096,1024]{1,0:T(8,128)(2,1)} fusion(bf16[4096,1024]{1,0:T(8,128)(2,1)} %param.11, s32[512]{0:T(512)S(1)} %copy-done.16, f32[512,1024]{1,0:T(8,128)} %get-tuple-element.64, f32[512]{0:T(512)S(1)} %bitcast.192), kind=kOutput, calls=%fused_computation.4 | convolution fusion | flops 4310695936 | bytes 18878464 | tf_op jit(solution)/shard_map/kt,kd->td/dot_general | solution.py:179
  514.4 11.7 %add_convert_fusion = bf16[4096,1024]{1,0:T(8,128)(2,1)} fusion(bf16[4096,1024]{1,0:T(8,128)(2,1)} %param.12, s32[512]{0:T(512)S(1)} %copy-done.16, f32[512,1024]{1,0:T(8,128)S(1)} %get-tuple-element.59, f32[512,1024]{1,0:T(8,128)S(1)} %copy-done.42, f32[1024]{0:T(1024)S(1)} %copy-done.19, f32[512]{0:T(512)S(1)} %copy-done.29, f32[512]{0:T(512)S(1)} %copy-done.32, ...), kind=kOutput, calls=%fused_computation | convolution fusion | flops 4316987392 | bytes 25190400 | tf_op jit(solution)/shard_map/kt,kd->td/dot_general | solution.py:247
  526.0 97.5 %all-reduce.3.cloned.1.call-done = (bf16[128,3072]{1,0:T(8,128)(2,1)}, bf16[128,1024]{1,0:T(8,128)(2,1)}, bf16[128,4096]{1,0:T(8,128)(2,1)}, bf16[512,1024]{1,0:T(8,128)(2,1)}) async-done(((bf16[128,3072]{1,0:T(8,128)(2,1)}, bf16[128,1024]{1,0:T(8,128)(2,1)}, bf16[128,4096]{1,0:T(8,128)(2,1)}, bf16[512,1024]{1,0:T(8,128)(2,1)}), (bf16[128,3072]{1,0:T(8,128)(2,1)}, bf16[128,1024]{1,0:T(8,128)(2,1)}, ...) | async-done | bytes 3145744 | tf_op jit(solution)/shard_map/psum | solution.py:107
  (222 shorter events, 121.6 us)
Async XLA Ops:
  7.2 50.9 %all-gather.7.cloned.1.call-start = ((), (), s32[]{:S(2)}) async-start(), calls=%async_computation | async-start | bytes 7077888 | tf_op jit(solution)/shard_map/all_gather | solution.py:134
  7.9 92.2 %all-gather.9.cloned.1.call-start = ((), (), s32[]{:S(2)}) async-start(), calls=%async_computation.1 | async-start | bytes 2359296 | tf_op jit(solution)/shard_map/all_gather | solution.py:137
  8.7 135.2 %all-gather.11.cloned.1.call-start = ((), (), s32[]{:S(2)}) async-start(), calls=%async_computation.2 | async-start | bytes 9437184 | tf_op jit(solution)/shard_map/all_gather | solution.py:139
  9.4 190.5 %all-gather.13.cloned.1.call-start = ((), (), s32[]{:S(2)}) async-start(), calls=%async_computation.3 | async-start | bytes 9437184 | tf_op jit(solution)/shard_map/all_gather | solution.py:142
  10.0 613.6 %all-reduce.3.cloned.1.call-start = ((), (), s32[]{:S(2)}) async-start(), calls=%async_computation.4 | async-start | bytes 6291456 | tf_op jit(solution)/shard_map/psum | solution.py:107
  23.3 34.8 %copy-start.20 = (f32[8,1,128]{2,1,0:T(1,128)}, f32[8,1,128]{2,1,0:T(1,128)S(1)}, u32[]{:S(2)}) copy-start(f32[8,1,128]{2,1,0:T(1,128)S(1)} %convert_element_type.306) | copy-start | bytes 12292
  32.1 203.1 %copy-start.22 = (f32[8,1,128]{2,1,0:T(1,128)}, f32[8,1,128]{2,1,0:T(1,128)S(1)}, u32[]{:S(2)}) copy-start(f32[8,1,128]{2,1,0:T(1,128)S(1)} %convert_element_type.307) | copy-start | bytes 12292
  41.4 193.8 %copy-start.26 = (f32[1,512]{1,0:T(1,128)}, f32[1,512]{1,0:T(1,128)S(1)}, u32[]{:S(2)}) copy-start(f32[1,512]{1,0:T(1,128)S(1)} %fusion.58) | copy-start | bytes 6148
  105.3 129.9 %copy-start.36 = (f32[512]{0:T(512)}, f32[512]{0:T(512)S(1)}, u32[]{:S(2)}) copy-start(f32[512]{0:T(512)S(1)} %fusion.85) | copy-start | bytes 6148
  245.6 80.9 %copy-start.28 = (f32[512]{0:T(512)}, f32[512]{0:T(512)S(1)}, u32[]{:S(2)}) copy-start(f32[512]{0:T(512)S(1)} %get-tuple-element.46) | copy-start | bytes 6148
  293.4 29.2 %collective-permute-start.5 = (bf16[4,128,1024]{2,1,0:T(8,128)(2,1)S(1)}, bf16[4,128,1024]{2,1,0:T(8,128)(2,1)}, u32[]{:S(2)}, u32[]{:S(2)}) collective-permute-start(bf16[4,128,1024]{2,1,0:T(8,128)(2,1)S(1)} %fusion.32), channel_id=1, source_target_pairs={{0,4},{4,0},{8,12},{12,8},{16,20},{20,16},{24,28},{28,24},{1,5},{5... | collective-permute-start | bytes 3145736 | tf_op jit(solution)/shard_map/ppermute | solution.py:80
  299.8 119.9 %collective-permute-start.15 = (bf16[4,512,1024]{2,1,0:T(8,128)(2,1)}, bf16[4,512,1024]{2,1,0:T(8,128)(2,1)}, u32[]{:S(2)}, u32[]{:S(2)}) collective-permute-start(bf16[4,512,1024]{2,1,0:T(8,128)(2,1)} %fusion.17), channel_id=1, source_target_pairs={{0,4},{4,0},{8,12},{12,8},{16,20},{20,16},{24,28},{28,24},{1,5},{5... | collective-permute-start | bytes 12582920 | tf_op jit(solution)/shard_map/ppermute | solution.py:80
  307.1 27.8 %collective-permute-start = (bf16[4,128,3072]{2,1,0:T(8,128)(2,1)}, bf16[4,128,3072]{2,1,0:T(8,128)(2,1)}, u32[]{:S(2)}, u32[]{:S(2)}) collective-permute-start(bf16[4,128,3072]{2,1,0:T(8,128)(2,1)} %fusion.22), channel_id=1, source_target_pairs={{0,4},{4,0},{8,12},{12,8},{16,20},{20,16},{24,28},{28,24},{1,5},{5... | collective-permute-start | bytes 9437192 | tf_op jit(solution)/shard_map/ppermute | solution.py:80
  313.4 98.5 %collective-permute-start.10 = (bf16[4,128,4096]{2,1,0:T(8,128)(2,1)}, bf16[4,128,4096]{2,1,0:T(8,128)(2,1)}, u32[]{:S(2)}, u32[]{:S(2)}) collective-permute-start(bf16[4,128,4096]{2,1,0:T(8,128)(2,1)} %fusion.16), channel_id=1, source_target_pairs={{0,4},{4,0},{8,12},{12,8},{16,20},{20,16},{24,28},{28,24},{1,5},{5... | collective-permute-start | bytes 12582920 | tf_op jit(solution)/shard_map/ppermute | solution.py:80
  324.4 8.5 %collective-permute-start.8 = (bf16[2,64,1024]{2,1,0:T(8,128)(2,1)S(1)}, bf16[2,64,1024]{2,1,0:T(8,128)(2,1)S(1)}, u32[]{:S(2)}, u32[]{:S(2)}) collective-permute-start(bf16[2,64,1024]{2,1,0:T(8,128)(2,1)S(1)} %pad_maximum_fusion.13), channel_id=1, source_target_pairs={{0,16},{4,20},{8,24},{12,28},{16,0},{20,4},{24,8},{28,12},{1,17},{... | collective-permute-start | bytes 786440 | tf_op jit(solution)/shard_map/ppermute | solution.py:93
  325.6 8.2 %collective-permute-start.6 = (bf16[2,64,1024]{2,1,0:T(8,128)(2,1)S(1)}, bf16[2,64,1024]{2,1,0:T(8,128)(2,1)S(1)}, u32[]{:S(2)}, u32[]{:S(2)}) collective-permute-start(bf16[2,64,1024]{2,1,0:T(8,128)(2,1)S(1)} %pad_maximum_fusion.12), channel_id=1, source_target_pairs={{0,8},{4,12},{8,0},{12,4},{16,24},{20,28},{24,16},{28,20},{1,9},{5... | collective-permute-start | bytes 786440 | tf_op jit(solution)/shard_map/ppermute | solution.py:90
  334.0 11.3 %collective-permute-start.7 = (bf16[64,1024]{1,0:T(8,128)(2,1)S(1)}, bf16[64,1024]{1,0:T(8,128)(2,1)S(1)}, u32[]{:S(2)}, u32[]{:S(2)}) collective-permute-start(bf16[64,1024]{1,0:T(8,128)(2,1)S(1)} %get-tuple-element.42), channel_id=1, source_target_pairs={{0,16},{4,20},{8,24},{12,28},{16,0},{20,4},{24,8},{28,12},{1,17},{... | collective-permute-start | bytes 393224 | tf_op jit(solution)/shard_map/ppermute | solution.py:100
  341.7 61.2 %collective-permute-start.3 = (bf16[2,64,3072]{2,1,0:T(8,128)(2,1)}, bf16[2,64,3072]{2,1,0:T(8,128)(2,1)}, u32[]{:S(2)}, u32[]{:S(2)}) collective-permute-start(bf16[2,64,3072]{2,1,0:T(8,128)(2,1)} %pad_maximum_fusion.10), channel_id=1, source_target_pairs={{0,16},{4,20},{8,24},{12,28},{16,0},{20,4},{24,8},{28,12},{1,17},{... | collective-permute-start | bytes 2359304 | tf_op jit(solution)/shard_map/ppermute | solution.py:93
  343.8 60.4 %collective-permute-start.1 = (bf16[2,64,3072]{2,1,0:T(8,128)(2,1)}, bf16[2,64,3072]{2,1,0:T(8,128)(2,1)}, u32[]{:S(2)}, u32[]{:S(2)}) collective-permute-start(bf16[2,64,3072]{2,1,0:T(8,128)(2,1)} %pad_maximum_fusion.9), channel_id=1, source_target_pairs={{0,8},{4,12},{8,0},{12,4},{16,24},{20,28},{24,16},{28,20},{1,9},{5... | collective-permute-start | bytes 2359304 | tf_op jit(solution)/shard_map/ppermute | solution.py:90
  345.3 55.7 %collective-permute-start.9 = (bf16[64,1024]{1,0:T(8,128)(2,1)S(1)}, bf16[64,1024]{1,0:T(8,128)(2,1)S(1)}, u32[]{:S(2)}, u32[]{:S(2)}) collective-permute-start(bf16[64,1024]{1,0:T(8,128)(2,1)S(1)} %get-tuple-element.43), channel_id=1, source_target_pairs={{0,8},{4,12},{8,0},{12,4},{16,24},{20,28},{24,16},{28,20},{1,9},{5... | collective-permute-start | bytes 393224 | tf_op jit(solution)/shard_map/ppermute | solution.py:103
  408.0 29.2 %collective-permute-start.2 = (bf16[64,3072]{1,0:T(8,128)(2,1)}, bf16[64,3072]{1,0:T(8,128)(2,1)S(1)}, u32[]{:S(2)}, u32[]{:S(2)}) collective-permute-start(bf16[64,3072]{1,0:T(8,128)(2,1)} %get-tuple-element.33), channel_id=1, source_target_pairs={{0,16},{4,20},{8,24},{12,28},{16,0},{20,4},{24,8},{28,12},{1,17},{... | collective-permute-start | bytes 1179656 | tf_op jit(solution)/shard_map/ppermute | solution.py:100
  410.7 27.8 %collective-permute-start.4 = (bf16[64,3072]{1,0:T(8,128)(2,1)}, bf16[64,3072]{1,0:T(8,128)(2,1)}, u32[]{:S(2)}, u32[]{:S(2)}) collective-permute-start(bf16[64,3072]{1,0:T(8,128)(2,1)} %get-tuple-element.34), channel_id=1, source_target_pairs={{0,8},{4,12},{8,0},{12,4},{16,24},{20,28},{24,16},{28,20},{1,9},{5... | collective-permute-start | bytes 1179656 | tf_op jit(solution)/shard_map/ppermute | solution.py:103
  433.7 26.1 %collective-permute-start.18 = (bf16[2,256,1024]{2,1,0:T(8,128)(2,1)S(1)}, bf16[2,256,1024]{2,1,0:T(8,128)(2,1)S(1)}, u32[]{:S(2)}, u32[]{:S(2)}) collective-permute-start(bf16[2,256,1024]{2,1,0:T(8,128)(2,1)S(1)} %pad_maximum_fusion.7), channel_id=1, source_target_pairs={{0,16},{4,20},{8,24},{12,28},{16,0},{20,4},{24,8},{28,12},{1,17},{... | collective-permute-start | bytes 3145736 | tf_op jit(solution)/shard_map/ppermute | solution.py:93
  434.3 26.1 %collective-permute-start.16 = (bf16[2,256,1024]{2,1,0:T(8,128)(2,1)S(1)}, bf16[2,256,1024]{2,1,0:T(8,128)(2,1)S(1)}, u32[]{:S(2)}, u32[]{:S(2)}) collective-permute-start(bf16[2,256,1024]{2,1,0:T(8,128)(2,1)S(1)} %pad_maximum_fusion.6), channel_id=1, source_target_pairs={{0,8},{4,12},{8,0},{12,4},{16,24},{20,28},{24,16},{28,20},{1,9},{5... | collective-permute-start | bytes 3145736 | tf_op jit(solution)/shard_map/ppermute | solution.py:90
  434.9 25.7 %slice-start = ((s8[8388608]{0:T(1024)(128)(4,1)}), s8[4194304]{0:T(1024)(128)(4,1)S(1)}, s32[]{:S(2)}) async-start(s8[8388608]{0:T(1024)(128)(4,1)} %bitcast.157), calls=%async_computation.5 | async-start | bytes 8388608
  435.0 47.3 %collective-permute-start.13 = (bf16[2,64,4096]{2,1,0:T(8,128)(2,1)S(1)}, bf16[2,64,4096]{2,1,0:T(8,128)(2,1)S(1)}, u32[]{:S(2)}, u32[]{:S(2)}) collective-permute-start(bf16[2,64,4096]{2,1,0:T(8,128)(2,1)S(1)} %pad_maximum_fusion.4), channel_id=1, source_target_pairs={{0,16},{4,20},{8,24},{12,28},{16,0},{20,4},{24,8},{28,12},{1,17},{... | collective-permute-start | bytes 3145736 | tf_op jit(solution)/shard_map/ppermute | solution.py:93
  437.2 23.4 %slice-start.1 = ((s8[8388608]{0:T(1024)(128)(4,1)}), s8[4194304]{0:T(1024)(128)(4,1)S(1)}, s32[]{:S(2)}) async-start(s8[8388608]{0:T(1024)(128)(4,1)} %bitcast.157), calls=%async_computation.6 | async-start | bytes 8388608
  437.2 45.6 %collective-permute-start.11 = (bf16[2,64,4096]{2,1,0:T(8,128)(2,1)S(1)}, bf16[2,64,4096]{2,1,0:T(8,128)(2,1)S(1)}, u32[]{:S(2)}, u32[]{:S(2)}) collective-permute-start(bf16[2,64,4096]{2,1,0:T(8,128)(2,1)S(1)} %pad_maximum_fusion.3), channel_id=1, source_target_pairs={{0,8},{4,12},{8,0},{12,4},{16,24},{20,28},{24,16},{28,20},{1,9},{5... | collective-permute-start | bytes 3145736 | tf_op jit(solution)/shard_map/ppermute | solution.py:90
  460.9 32.6 %collective-permute-start.17 = (bf16[256,1024]{1,0:T(8,128)(2,1)S(1)}, bf16[256,1024]{1,0:T(8,128)(2,1)S(1)}, u32[]{:S(2)}, u32[]{:S(2)}) collective-permute-start(bf16[256,1024]{1,0:T(8,128)(2,1)S(1)} %get-tuple-element.21), channel_id=1, source_target_pairs={{0,16},{4,20},{8,24},{12,28},{16,0},{20,4},{24,8},{28,12},{1,17},{... | collective-permute-start | bytes 1572872 | tf_op jit(solution)/shard_map/ppermute | solution.py:100
  462.6 31.4 %collective-permute-start.19 = (bf16[256,1024]{1,0:T(8,128)(2,1)S(1)}, bf16[256,1024]{1,0:T(8,128)(2,1)S(1)}, u32[]{:S(2)}, u32[]{:S(2)}) collective-permute-start(bf16[256,1024]{1,0:T(8,128)(2,1)S(1)} %get-tuple-element.22), channel_id=1, source_target_pairs={{0,8},{4,12},{8,0},{12,4},{16,24},{20,28},{24,16},{28,20},{1,9},{5... | collective-permute-start | bytes 1572872 | tf_op jit(solution)/shard_map/ppermute | solution.py:103
  483.3 18.3 %collective-permute-start.12 = (bf16[64,4096]{1,0:T(8,128)(2,1)S(1)}, bf16[64,4096]{1,0:T(8,128)(2,1)S(1)}, u32[]{:S(2)}, u32[]{:S(2)}) collective-permute-start(bf16[64,4096]{1,0:T(8,128)(2,1)S(1)} %get-tuple-element.27), channel_id=1, source_target_pairs={{0,16},{4,20},{8,24},{12,28},{16,0},{20,4},{24,8},{28,12},{1,17},{... | collective-permute-start | bytes 1572872 | tf_op jit(solution)/shard_map/ppermute | solution.py:100
  485.0 17.7 %collective-permute-start.14 = (bf16[64,4096]{1,0:T(8,128)(2,1)S(1)}, bf16[64,4096]{1,0:T(8,128)(2,1)S(1)}, u32[]{:S(2)}, u32[]{:S(2)}) collective-permute-start(bf16[64,4096]{1,0:T(8,128)(2,1)S(1)} %get-tuple-element.28), channel_id=1, source_target_pairs={{0,8},{4,12},{8,0},{12,4},{16,24},{20,28},{24,16},{28,20},{1,9},{5... | collective-permute-start | bytes 1572872 | tf_op jit(solution)/shard_map/ppermute | solution.py:103
  (41 other events, 360.2 us)
Sparse Core Ops, SparseCore 0:
  9.9 48.1 all-gather.6
  59.9 27.7 all-gather.8
  89.6 54.2 all-gather.10
  145.6 54.2 all-gather.12
  504.3 119.2 all-reduce.2
where the time goes:
time: 649 us; the launch traced here: 639 us
  waiting for transfers between devices  241 us (37%)
  matrix products  177 us (27%)
  other arithmetic  71.4 us (11%)
  blocking collectives  71.3 us (11%)
  local copies, waits for them, and re-layouts  43.3 us (7%)
  starting transfers between devices  20.8 us (3%)
  between operations  15.1 us (2%)
    psum x1, waiting for transfers between devices, plane_reduce(): return lax.psum(shard.astype(jnp.bfloat16), 'dp').astype(jnp.float32)  97.5 us
    psum x1, blocking collectives, per_device(): lax.psum(jnp.concatenate([grad_gain_one, grad_gain_two, router_local]), (...  52 us
    ppermute x4, waiting for transfers between devices, plane_reduce(): lax.ppermute(jnp.stack([to_y[half:], to_d[half:]]).astype(jnp.bfloat16),...  43.7 us
    all_gather x1, waiting for transfers between devices, per_device(): lax.all_gather(mlp_in, 'fsdp', axis=0, tiled=True)  38.6 us
    all_gather x1, waiting for transfers between devices, per_device(): w_down = lax.all_gather(mlp_out, 'fsdp', axis=0, tiled=True)  35.3 us
    add x4, other arithmetic, plane_reduce(): chip = keep + got.astype(jnp.float32)  20.5 us
    convert_element_type x4, local copies, waits for them, and re-layouts, plane_reduce(): got = lax.ppermute(send.astype(jnp.bfloat16), 'fsdp', swap_pairs(1, 8))  14.3 us
    dot_general x1, matrix products, per_device(): jnp.einsum('kd,fd->kf', grad_expanded, w_down, preferred_element_type=jnp...  13.3 us
  transfers between devices with their start and end apart: 25, of which 14 were waited for; matrix products, arithmetic and copies ran while one was open for 28% of the time, Pallas kernels for 0%

commit v1 on v0

--- a/solution.py
+++ b/solution.py
@@ -104,7 +104,7 @@
         jnp.float32
     )
     shard = jnp.concatenate([own_a + second_y, own_b + second_x], axis=0)
-    return lax.psum(shard.astype(jnp.bfloat16), "dp").astype(jnp.float32)
+    return jnp.sum(lax.all_gather(shard.astype(jnp.bfloat16), "dp"), axis=0).astype(jnp.float32)
 
 
 def plain_reduce(grad):

time: 649 us -> 607 us (0.935)
  waiting for transfers between devices: 241 us -> 207 us
  blocking collectives: 71.3 us -> 63.2 us
  other arithmetic: 71.4 us -> 78.9 us
  local copies, waits for them, and re-layouts: 43.3 us -> 36.7 us
    psum x1 -> x0, waiting for transfers between devices: 97.5 us -> none  [plane_reduce(): return lax.psum(shard.astype(jnp.bfloat16), 'dp').astype(jnp.float32)]
    all_gather x0 -> x4, waiting for transfers between devices: none -> 53.7 us  [plane_reduce(): lax.all_gather(shard.astype(jnp.bfloat16), 'dp')]
    reduce_sum x0 -> x4, other arithmetic: none -> 10.4 us  [plane_reduce(): jnp.sum(lax.all_gather(shard.astype(jnp.bfloat16), 'dp'), axis=0)]
    all_gather x1, waiting for transfers between devices: 35.3 us -> 44 us  [per_device(): w_down = lax.all_gather(mlp_out, 'fsdp', axis=0, tiled=True)]
    psum x1, blocking collectives: 52 us -> 43.9 us  [per_device(): lax.psum(jnp.concatenate([grad_gain_one, grad_gain_two, router_local]), (...]
    concatenate x4 -> x8, other arithmetic: 3.81 us -> 10.6 us  [plane_reduce(): shard = jnp.concatenate([own_a + second_y, own_b + second_x], axis=0)]
  transfers between devices with their start and end apart: 25 -> 28, of which waited for: 14 -> 15; matrix products, arithmetic and copies ran while one was open for 28% -> 33% of each run, Pallas kernels for 0% -> 0%
where the time goes in v1:
time: 607 us; the launch traced here: 598 us
  waiting for transfers between devices  207 us (34%)
  matrix products  179 us (29%)
  other arithmetic  78.9 us (13%)
  blocking collectives  63.2 us (10%)
  local copies, waits for them, and re-layouts  36.7 us (6%)
  starting transfers between devices  18.7 us (3%)
  between operations  15.1 us (2%)
    all_gather x4, waiting for transfers between devices, plane_reduce(): lax.all_gather(shard.astype(jnp.bfloat16), 'dp')  53.7 us
    ppermute x4, waiting for transfers between devices, plane_reduce(): lax.ppermute(jnp.stack([to_y[half:], to_d[half:]]).astype(jnp.bfloat16),...  46.5 us
    all_gather x1, waiting for transfers between devices, per_device(): w_down = lax.all_gather(mlp_out, 'fsdp', axis=0, tiled=True)  44 us
    psum x1, blocking collectives, per_device(): lax.psum(jnp.concatenate([grad_gain_one, grad_gain_two, router_local]), (...  43.9 us
    all_gather x1, waiting for transfers between devices, per_device(): lax.all_gather(mlp_in, 'fsdp', axis=0, tiled=True)  38.7 us
    add x4, other arithmetic, plane_reduce(): chip = keep + got.astype(jnp.float32)  16.7 us
    dot_general x1, matrix products, per_device(): jnp.einsum('kd,fd->kf', grad_expanded, w_down, preferred_element_type=jnp...  14.6 us
    dot_general x1, matrix products, per_device(): jnp.einsum('qhd,khd->hqk', grad_mix_heads, value_heads, preferred_element...  12.8 us
  transfers between devices with their start and end apart: 28, of which 15 were waited for; matrix products, arithmetic and copies ran while one was open for 33% of the time, Pallas kernels for 0%

profile of v1, /device:TPU:0, one launch (start us, length us, event | category | flops | bytes accessed | tf_op | source)
XLA Modules:
  0.0 598.0 jit_solution(11290603815287356935)
XLA Ops:
  10.9 10.4 %all-gather = bf16[8,1,128]{2,1,0:T(2,128)(2,1)S(1)} all-gather(bf16[1,1,128]{2,1,0:T(2,128)(2,1)} %bitcast.224), channel_id=1, replica_groups=mesh['fsdp'=8,'dp'=4] {'fsdp'}, dimensions={0}, use_global_device_ids=true | all-gather | bytes 2304 | tf_op jit(solution)/shard_map/all_gather | solution.py:135
  21.3 8.9 %all-gather.1 = bf16[8,1,128]{2,1,0:T(2,128)(2,1)S(1)} all-gather(bf16[1,1,128]{2,1,0:T(2,128)(2,1)} %bitcast.225), channel_id=1, replica_groups=mesh['fsdp'=8,'dp'=4] {'fsdp'}, dimensions={0}, use_global_device_ids=true | all-gather | bytes 2304 | tf_op jit(solution)/shard_map/all_gather | solution.py:140
  31.7 8.0 %multiply_reduce_fusion.7 = (f32[512]{0:T(512)S(1)}, f32[512,1024]{1,0:T(8,128)S(1)}) fusion(bf16[4096,1024]{1,0:T(8,128)(2,1)} %param.11, s32[512]{0:T(512)} %param.14), kind=kOutput, calls=%fused_computation.64 | convolution fusion | flops 4298112512 | bytes 10489856 | tf_op jit(solution)/shard_map/dot_general | solution.py:147
  40.4 9.3 %fusion.12 = f32[512,1024]{1,0:T(8,128)} fusion(bf16[4096,1024]{1,0:T(8,128)(2,1)} %param.12, s32[512]{0:T(512)S(1)} %copy-done.22), kind=kOutput, calls=%fused_computation.28 | convolution fusion | flops 4297064448 | bytes 10487808 | tf_op jit(solution)/shard_map/dot_general | solution.py:181
  49.6 8.4 %all-gather.11.cloned.1.call-done = bf16[1024,3072]{1,0:T(8,128)(2,1)} async-done(((bf16[128,3072]{1,0:T(8,128)(2,1)}), bf16[1024,3072]{1,0:T(8,128)(2,1)}) %all-gather.11.cloned.1.call-update) | async-done | bytes 6291472 | tf_op jit(solution)/shard_map/all_gather | solution.py:134
  58.0 6.6 %convolution_convert_fusion = bf16[512,3072]{1,0:T(8,128)(2,1)S(1)} fusion(bf16[1024,3072]{1,0:T(8,128)(2,1)} %all-gather.11.cloned.1.call-done, f32[512,1024]{1,0:T(8,128)S(1)} %get-tuple-element.55, f32[1024]{0:T(1024)S(1)} %bitcast.210, f32[512]{0:T(512)S(1)} %fusion.92), kind=kOutput, calls=%fused_computation.34 | convolution fusion | flops 3224371200 | bytes 11540480 | tf_op jit(solution)/shard_map/dot_general | solution.py:153
  72.4 8.8 %fusion.1 = (f32[16,512]{1,0:T(8,128)S(1)}, f32[16,512,512]{1,2,0:T(8,128)}) fusion(pred[512,512]{0,1:T(8,128)(4,1)S(1)} %compare_and_fusion, bf16[512,16,64]{0,2,1:T(8,128)(2,1)} %bitcast.191, bf16[512,16,64]{0,2,1:T(8,128)(2,1)S(1)} %bitcast.189), kind=kOutput, calls=%fused_computation.11 | convolution fusion | flops 549445632 | bytes 19169280 | tf_op jit(solution)/shard_map/qhd,khd->hqk/dot_general | solution.py:29
  81.3 9.3 %fusion = f32[16,512]{1,0:T(8,128)S(1)} fusion(f32[16,512,512]{1,2,0:T(8,128)} %get-tuple-element.57, f32[16,512]{1,0:T(8,128)S(1)} %get-tuple-element.56, pred[512,512]{0,1:T(8,128)(4,1)S(1)} %compare_and_fusion), kind=kLoop, calls=%fused_computation.8 | loop fusion | flops 16769024 | bytes 17104896 | tf_op jit(solution)/shard_map/reduce_sum | solution.py:160
  90.6 9.4 %fusion.26 = bf16[16,64,512]{2,1,0:T(8,128)(2,1)} fusion(bf16[512,16,64]{0,2,1:T(8,128)(2,1)} %bitcast.205, f32[16,512,512]{1,2,0:T(8,128)} %get-tuple-element.57, f32[16,512]{1,0:T(8,128)S(1)} %fusion, f32[16,512]{1,0:T(8,128)S(1)} %get-tuple-element.56, pred[512,512]{0,1:T(8,128)(4,1)S(1)} %compare_and_fusion), kind=kOutput, calls=%fused_computation.68 | convolution fusion | flops 558366720 | bytes 19202048 | tf_op jit(solution)/shard_map/hqk,khd->qhd/dot_general | solution.py:163
  105.2 38.7 %all-gather.15.cloned.1.call-done = bf16[1024,4096]{1,0:T(8,128)(2,1)} async-done(((bf16[128,4096]{1,0:T(8,128)(2,1)}), bf16[1024,4096]{1,0:T(8,128)(2,1)}) %all-gather.15.cloned.1.call-update) | async-done | bytes 8388624 | tf_op jit(solution)/shard_map/all_gather | solution.py:139
  143.9 12.1 %fusion.104 = f32[512,4096]{1,0:T(8,128)} fusion(bf16[1024,4096]{1,0:T(8,128)(2,1)} %all-gather.15.cloned.1.call-done, f32[512,1024]{1,0:T(8,128)} %get-tuple-element.14, f32[1024]{0:T(1024)S(1)} %bitcast.214, f32[512]{0:T(512)S(1)} %fusion.93), kind=kOutput, calls=%fused_computation.189 | convolution fusion | flops 4296540160 | bytes 18880512 | tf_op jit(solution)/shard_map/dot_general | solution.py:171
  156.0 44.0 %all-gather.17.cloned.1.call-done = bf16[4096,1024]{1,0:T(8,128)(2,1)} async-done(((bf16[512,1024]{1,0:T(8,128)(2,1)}), bf16[4096,1024]{1,0:T(8,128)(2,1)}) %all-gather.17.cloned.1.call-update) | async-done | bytes 8388624 | tf_op jit(solution)/shard_map/all_gather | solution.py:142
  199.9 14.6 %fusion.8 = bf16[512,4096]{1,0:T(8,128)(2,1)} fusion(f32[512,4096]{1,0:T(8,128)} %fusion.104, bf16[4096,1024]{1,0:T(8,128)(2,1)} %all-gather.17.cloned.1.call-done, f32[512,1024]{1,0:T(8,128)} %fusion.12, f32[512]{0:T(512)S(1)} %bitcast.219), kind=kOutput, calls=%fused_computation.18 | convolution fusion | flops 4337958912 | bytes 23070720 | tf_op jit(solution)/shard_map/kd,fd->kf/dot_general | solution.py:189
  214.6 10.9 %multiply_reduce_fusion.1 = (f32[1024]{0:T(1024)S(1)}, f32[512]{0:T(512)S(1)}, f32[512,1024]{1,0:T(8,128)}) fusion(f32[512,1024]{1,0:T(8,128)S(1)} %copy-done.10, f32[512]{0:T(512)S(1)} %fusion.93, f32[1024]{0:T(1024)S(1)} %bitcast.215, bf16[512,4096]{1,0:T(8,128)(2,1)} %fusion.8, bf16[1024,4096]{1,0:T(8,128)(2,1)} %all-gather.15.cloned.1.call-done), kind=kOutput, calls=%fused_computation.49 | convolution fusion | flops 4298111488 | bytes 16789504 | tf_op jit(solution)/shard_map/kf,df->kd/dot_general | solution.py:198
  225.5 10.3 %multiply_reduce_fusion.3 = (f32[512]{0:T(512)S(1)}, bf16[512,1024]{1,0:T(8,128)(2,1)S(1)}, f32[512,1024]{1,0:T(8,128)}) fusion(f32[512,1024]{1,0:T(8,128)S(1)} %copy-done.30, f32[512,1024]{1,0:T(8,128)S(1)} %copy-done.10, f32[512]{0:T(512)S(1)} %multiply_multiply_fusion.3, f32[512]{0:T(512)S(1)} %fusion.93, f32[512,1024]{1,0:T(8,128)} %get-tuple-element.59, ...), kind=kOutput, calls=%fused_computation.54 | convolution fusion | flops 4319608320 | bytes 28323840 | tf_op jit(solution)/shard_map/dot_general | solution.py:174
  241.4 10.6 %fusion.27 = bf16[16,64,512]{2,1,0:T(8,128)(2,1)S(1)} fusion(bf16[512,16,64]{0,2,1:T(8,128)(2,1)} %bitcast.207, f32[16,512]{1,0:T(8,128)S(1)} %log_add_fusion, f32[16,512,512]{1,2,0:T(8,128)} %get-tuple-element.57, pred[512,512]{0,1:T(8,128)(4,1)S(1)} %compare_and_fusion), kind=kOutput, calls=%fused_computation.70 | convolution fusion | flops 558366720 | bytes 19169280 | tf_op jit(solution)/shard_map/hqk,qhd->khd/dot_general | solution.py:227
  252.0 12.8 %multiply_reduce_fusion = (f32[16,512]{1,0:T(8,128)S(1)}, f32[16,512,512]{1,2,0:T(8,128)}) fusion(f32[16,512]{1,0:T(8,128)S(1)} %log_add_fusion, f32[16,512,512]{1,2,0:T(8,128)} %get-tuple-element.57, pred[512,512]{0,1:T(8,128)(4,1)S(1)} %compare_and_fusion, bf16[512,16,64]{0,2,1:T(8,128)(2,1)S(1)} %bitcast.208, bf16[512,16,64]{0,2,1:T(8,128)(2,1)S(1)} %bitcast.206), kind=kOutput, calls=%fused_computation.2 | convolution fusion | flops 562028544 | bytes 35979264 | tf_op jit(solution)/shard_map/qhd,khd->hqk/dot_general | solution.py:213
  264.8 12.6 %multiply_convert_fusion = bf16[16,512,512]{1,2,0:T(8,128)(2,1)S(1)} fusion(f32[16,512,512]{1,2,0:T(8,128)} %get-tuple-element.62, f32[16,512]{1,0:T(8,128)S(1)} %get-tuple-element.61, f32[16,512]{1,0:T(8,128)S(1)} %log_add_fusion, f32[16,512,512]{1,2,0:T(8,128)} %get-tuple-element.57, pred[512,512]{0,1:T(8,128)(4,1)S(1)} %compare_and_fusion), kind=kLoop, calls=%fused_computation.1 | loop fusion | flops 29360128 | bytes 42270720 | tf_op jit(solution)/shard_map/convert_element_type | solution.py:217
  295.2 9.1 %fusion.101 = f32[4096,1024]{1,0:T(8,128)S(1)} fusion(f32[512,1024]{1,0:T(8,128)} %fusion.12, f32[512]{0:T(512)S(1)} %bitcast.221, f32[512,4096]{1,0:T(8,128)} %fusion.104), kind=kOutput, calls=%fused_computation.186 | convolution fusion | flops 4314890240 | bytes 27265024 | tf_op jit(solution)/shard_map/kf,kd->fd/dot_general | solution.py:185
  321.6 8.2 %fusion.103 = f32[1024,4096]{1,0:T(8,128)} fusion(bf16[512,4096]{1,0:T(8,128)(2,1)S(1)} %copy-done.29, f32[512,1024]{1,0:T(8,128)S(1)} %copy-done.11, f32[1024]{0:T(1024)S(1)} %bitcast.217, f32[512]{0:T(512)S(1)} %fusion.93), kind=kOutput, calls=%fused_computation.188 | convolution fusion | flops 4296540160 | bytes 23074816 | tf_op jit(solution)/shard_map/kd,kf->df/dot_general | solution.py:194
  330.7 5.9 collective-permute-done.3
  344.7 6.0 %fusion.16 = bf16[4,128,4096]{2,1,0:T(8,128)(2,1)} fusion(f32[4,2,128,4096]{3,2,1,0:T(8,128)} %bitcast.195, s32[]{:T(128)S(6)} %select_n.98), kind=kLoop, calls=%fused_computation.35 | loop fusion | bytes 8388612 | tf_op jit(solution)/shard_map/convert_element_type | solution.py:80
  356.9 6.0 %bitcast_add_fusion = f32[4,512,1024]{2,1,0:T(8,128)S(1)} fusion(bf16[4,512,1024]{2,1,0:T(8,128)(2,1)} %collective-permute-done.15, f32[4,2,512,1024]{3,2,1,0:T(8,128)} %bitcast.194, s32[]{:T(128)S(6)} %select_n.97), kind=kLoop, calls=%fused_computation.21 | loop fusion | flops 4194304 | bytes 20971524 | tf_op jit(solution)/shard_map/add | solution.py:81
  365.3 21.0 %collective-permute-done.18 = bf16[2,256,1024]{2,1,0:T(8,128)(2,1)S(1)} collective-permute-done((bf16[2,256,1024]{2,1,0:T(8,128)(2,1)S(1)}, bf16[2,256,1024]{2,1,0:T(8,128)(2,1)S(1)}, u32[]{:S(2)}, u32[]{:S(2)}) %collective-permute-start.18) | collective-permute-done | bytes 1048608 | tf_op jit(solution)/shard_map/ppermute | solution.py:93
  391.1 5.8 bitcast_add_fusion.1
  409.4 19.5 %collective-permute-done.13 = bf16[2,64,4096]{2,1,0:T(8,128)(2,1)S(1)} collective-permute-done((bf16[2,64,4096]{2,1,0:T(8,128)(2,1)S(1)}, bf16[2,64,4096]{2,1,0:T(8,128)(2,1)S(1)}, u32[]{:S(2)}, u32[]{:S(2)}) %collective-permute-start.13) | collective-permute-done | bytes 1048608 | tf_op jit(solution)/shard_map/ppermute | solution.py:93
  434.3 6.9 %collective-permute-done.12 = bf16[64,4096]{1,0:T(8,128)(2,1)S(1)} collective-permute-done((bf16[64,4096]{1,0:T(8,128)(2,1)S(1)}, bf16[64,4096]{1,0:T(8,128)(2,1)S(1)}, u32[]{:S(2)}, u32[]{:S(2)}) %collective-permute-start.12) | collective-permute-done | bytes 524320 | tf_op jit(solution)/shard_map/ppermute | solution.py:100
  446.5 8.4 %multiply_reduce_fusion.2 = (f32[1024]{0:T(1024)S(1)}, f32[512]{0:T(512)S(1)}, f32[512,1024]{1,0:T(8,128)}) fusion(f32[512,1024]{1,0:T(8,128)S(1)} %get-tuple-element.55, f32[512]{0:T(512)S(1)} %fusion.92, f32[1024]{0:T(1024)S(1)} %bitcast.212, bf16[1024,3072]{1,0:T(8,128)(2,1)} %all-gather.11.cloned.1.call-done, bf16[512,1024]{0,1:T(8,128)(2,1)} %bitcast.229, ...), kind=kOutput, calls=%fused_computation.50 | convolution fusion | flops 3233806848 | bytes 13643776 | tf_op jit(solution)/shard_map/ke,de->kd/dot_general | solution.py:240
  454.9 43.9 %psum.7 = f32[3072]{0:T(1024)S(1)} all-reduce(f32[3072]{0:T(1024)S(1)} %pad_maximum_fusion.15), channel_id=1, replica_groups=mesh['fsdp'=8,'dp'=4] {'fsdp','dp'}, use_global_device_ids=true, to_apply=%region_16.17 | all-reduce | flops 3072 | bytes 24576 | tf_op jit(solution)/shard_map/psum | solution.py:250
  500.1 10.0 %add_convert_fusion.1 = bf16[4096,1024]{1,0:T(8,128)(2,1)} fusion(bf16[4096,1024]{1,0:T(8,128)(2,1)} %param.11, s32[512]{0:T(512)S(1)} %copy-done.23, f32[512,1024]{1,0:T(8,128)} %get-tuple-element.60, f32[512]{0:T(512)S(1)} %bitcast.222), kind=kOutput, calls=%fused_computation.4 | convolution fusion | flops 4310695936 | bytes 18878464 | tf_op jit(solution)/shard_map/kt,kd->td/dot_general | solution.py:179
  510.2 11.5 %add_convert_fusion = bf16[4096,1024]{1,0:T(8,128)(2,1)} fusion(bf16[4096,1024]{1,0:T(8,128)(2,1)} %param.12, s32[512]{0:T(512)S(1)} %copy-done.23, f32[512,1024]{1,0:T(8,128)S(1)} %get-tuple-element.55, f32[512,1024]{1,0:T(8,128)S(1)} %copy-done.31, f32[1024]{0:T(1024)S(1)} %convert_element_type.291, f32[512]{0:T(512)S(1)} %get-tuple-element.42, ...), kind=kOutput, calls=%fused_computation | convolution fusion | flops 4316987392 | bytes 25190400 | tf_op jit(solution)/shard_map/kt,kd->td/dot_general | solution.py:247
  532.7 53.7 %all-gather.23.cloned.1.call-done = bf16[4,128,4096]{2,1,0:T(8,128)(2,1)} async-done(((bf16[1,128,4096]{2,1,0:T(8,128)(2,1)}), bf16[4,128,4096]{2,1,0:T(8,128)(2,1)}) %all-gather.23.cloned.1.call-update) | async-done | bytes 4194320 | tf_op jit(solution)/shard_map/all_gather | solution.py:107
  (203 shorter events, 121.2 us)
Async XLA Ops:
  7.2 50.9 %all-gather.11.cloned.1.call-start = ((), (), s32[]{:S(2)}) async-start(), calls=%async_computation | async-start | bytes 7077888 | tf_op jit(solution)/shard_map/all_gather | solution.py:134
  7.9 92.1 %all-gather.13.cloned.1.call-start = ((), (), s32[]{:S(2)}) async-start(), calls=%async_computation.1 | async-start | bytes 2359296 | tf_op jit(solution)/shard_map/all_gather | solution.py:137
  8.7 135.2 %all-gather.15.cloned.1.call-start = ((), (), s32[]{:S(2)}) async-start(), calls=%async_computation.2 | async-start | bytes 9437184 | tf_op jit(solution)/shard_map/all_gather | solution.py:139
  9.4 190.5 %all-gather.17.cloned.1.call-start = ((), (), s32[]{:S(2)}) async-start(), calls=%async_computation.3 | async-start | bytes 9437184 | tf_op jit(solution)/shard_map/all_gather | solution.py:142
  10.0 511.7 %all-gather.21.cloned.1.call-start = ((), (), s32[]{:S(2)}) async-start(), calls=%async_computation.5 | async-start | bytes 1310720 | tf_op jit(solution)/shard_map/all_gather | solution.py:107
  252.0 31.8 %copy-start.28 = (bf16[16,64,512]{2,1,0:T(8,128)(2,1)}, bf16[16,64,512]{2,1,0:T(8,128)(2,1)S(1)}, u32[]{:S(2)}) copy-start(bf16[16,64,512]{2,1,0:T(8,128)(2,1)S(1)} %fusion.27) | copy-start | bytes 3145732
  283.4 6.7 %collective-permute-start.5 = (bf16[4,128,1024]{2,1,0:T(8,128)(2,1)S(1)}, bf16[4,128,1024]{2,1,0:T(8,128)(2,1)S(1)}, u32[]{:S(2)}, u32[]{:S(2)}) collective-permute-start(bf16[4,128,1024]{2,1,0:T(8,128)(2,1)S(1)} %fusion.32), channel_id=1, source_target_pairs={{0,4},{4,0},{8,12},{12,8},{16,20},{20,16},{24,28},{28,24},{1,5},{5... | collective-permute-start | bytes 3145736 | tf_op jit(solution)/shard_map/ppermute | solution.py:80
  289.9 21.4 %collective-permute-start = (bf16[4,128,3072]{2,1,0:T(8,128)(2,1)}, bf16[4,128,3072]{2,1,0:T(8,128)(2,1)}, u32[]{:S(2)}, u32[]{:S(2)}) collective-permute-start(bf16[4,128,3072]{2,1,0:T(8,128)(2,1)} %fusion.22), channel_id=1, source_target_pairs={{0,4},{4,0},{8,12},{12,8},{16,20},{20,16},{24,28},{28,24},{1,5},{5... | collective-permute-start | bytes 9437192 | tf_op jit(solution)/shard_map/ppermute | solution.py:80
  293.0 14.5 %collective-permute-start.8 = (bf16[2,64,1024]{2,1,0:T(8,128)(2,1)S(1)}, bf16[2,64,1024]{2,1,0:T(8,128)(2,1)S(1)}, u32[]{:S(2)}, u32[]{:S(2)}) collective-permute-start(bf16[2,64,1024]{2,1,0:T(8,128)(2,1)S(1)} %pad_maximum_fusion.13), channel_id=1, source_target_pairs={{0,16},{4,20},{8,24},{12,28},{16,0},{20,4},{24,8},{28,12},{1,17},{... | collective-permute-start | bytes 786440 | tf_op jit(solution)/shard_map/ppermute | solution.py:93
  294.2 13.3 %collective-permute-start.6 = (bf16[2,64,1024]{2,1,0:T(8,128)(2,1)S(1)}, bf16[2,64,1024]{2,1,0:T(8,128)(2,1)S(1)}, u32[]{:S(2)}, u32[]{:S(2)}) collective-permute-start(bf16[2,64,1024]{2,1,0:T(8,128)(2,1)S(1)} %pad_maximum_fusion.12), channel_id=1, source_target_pairs={{0,8},{4,12},{8,0},{12,4},{16,24},{20,28},{24,16},{28,20},{1,9},{5... | collective-permute-start | bytes 786440 | tf_op jit(solution)/shard_map/ppermute | solution.py:90
  307.5 49.4 %collective-permute-start.15 = (bf16[4,512,1024]{2,1,0:T(8,128)(2,1)}, bf16[4,512,1024]{2,1,0:T(8,128)(2,1)}, u32[]{:S(2)}, u32[]{:S(2)}) collective-permute-start(bf16[4,512,1024]{2,1,0:T(8,128)(2,1)} %fusion.17), channel_id=1, source_target_pairs={{0,4},{4,0},{8,12},{12,8},{16,20},{20,16},{24,28},{28,24},{1,5},{5... | collective-permute-start | bytes 12582920 | tf_op jit(solution)/shard_map/ppermute | solution.py:80
  307.7 22.1 %collective-permute-start.7 = (bf16[64,1024]{1,0:T(8,128)(2,1)S(1)}, bf16[64,1024]{1,0:T(8,128)(2,1)S(1)}, u32[]{:S(2)}, u32[]{:S(2)}) collective-permute-start(bf16[64,1024]{1,0:T(8,128)(2,1)S(1)} %get-tuple-element.38), channel_id=1, source_target_pairs={{0,16},{4,20},{8,24},{12,28},{16,0},{20,4},{24,8},{28,12},{1,17},{... | collective-permute-start | bytes 393224 | tf_op jit(solution)/shard_map/ppermute | solution.py:100
  309.3 20.5 %collective-permute-start.9 = (bf16[64,1024]{1,0:T(8,128)(2,1)S(1)}, bf16[64,1024]{1,0:T(8,128)(2,1)S(1)}, u32[]{:S(2)}, u32[]{:S(2)}) collective-permute-start(bf16[64,1024]{1,0:T(8,128)(2,1)S(1)} %get-tuple-element.39), channel_id=1, source_target_pairs={{0,8},{4,12},{8,0},{12,4},{16,24},{20,28},{24,16},{28,20},{1,9},{5... | collective-permute-start | bytes 393224 | tf_op jit(solution)/shard_map/ppermute | solution.py:103
  317.2 19.5 %collective-permute-start.3 = (bf16[2,64,3072]{2,1,0:T(8,128)(2,1)}, bf16[2,64,3072]{2,1,0:T(8,128)(2,1)}, u32[]{:S(2)}, u32[]{:S(2)}) collective-permute-start(bf16[2,64,3072]{2,1,0:T(8,128)(2,1)} %pad_maximum_fusion.10), channel_id=1, source_target_pairs={{0,16},{4,20},{8,24},{12,28},{16,0},{20,4},{24,8},{28,12},{1,17},{... | collective-permute-start | bytes 2359304 | tf_op jit(solution)/shard_map/ppermute | solution.py:93
  319.6 19.2 %collective-permute-start.1 = (bf16[2,64,3072]{2,1,0:T(8,128)(2,1)}, bf16[2,64,3072]{2,1,0:T(8,128)(2,1)}, u32[]{:S(2)}, u32[]{:S(2)}) collective-permute-start(bf16[2,64,3072]{2,1,0:T(8,128)(2,1)} %pad_maximum_fusion.9), channel_id=1, source_target_pairs={{0,8},{4,12},{8,0},{12,4},{16,24},{20,28},{24,16},{28,20},{1,9},{5... | collective-permute-start | bytes 2359304 | tf_op jit(solution)/shard_map/ppermute | solution.py:90
  330.6 193.3 %all-gather.19.cloned.1.call-start = ((), (), s32[]{:S(2)}) async-start(), calls=%async_computation.4 | async-start | bytes 3932160 | tf_op jit(solution)/shard_map/all_gather | solution.py:107
  343.0 9.8 %collective-permute-start.2 = (bf16[64,3072]{1,0:T(8,128)(2,1)}, bf16[64,3072]{1,0:T(8,128)(2,1)S(1)}, u32[]{:S(2)}, u32[]{:S(2)}) collective-permute-start(bf16[64,3072]{1,0:T(8,128)(2,1)} %get-tuple-element.29), channel_id=1, source_target_pairs={{0,16},{4,20},{8,24},{12,28},{16,0},{20,4},{24,8},{28,12},{1,17},{... | collective-permute-start | bytes 1179656 | tf_op jit(solution)/shard_map/ppermute | solution.py:100
  344.2 9.6 %collective-permute-start.4 = (bf16[64,3072]{1,0:T(8,128)(2,1)S(1)}, bf16[64,3072]{1,0:T(8,128)(2,1)S(1)}, u32[]{:S(2)}, u32[]{:S(2)}) collective-permute-start(bf16[64,3072]{1,0:T(8,128)(2,1)S(1)} %get-tuple-element.30), channel_id=1, source_target_pairs={{0,8},{4,12},{8,0},{12,4},{16,24},{20,28},{24,16},{28,20},{1,9},{5... | collective-permute-start | bytes 1179656 | tf_op jit(solution)/shard_map/ppermute | solution.py:103
  350.8 40.4 %collective-permute-start.10 = (bf16[4,128,4096]{2,1,0:T(8,128)(2,1)}, bf16[4,128,4096]{2,1,0:T(8,128)(2,1)}, u32[]{:S(2)}, u32[]{:S(2)}) collective-permute-start(bf16[4,128,4096]{2,1,0:T(8,128)(2,1)} %fusion.16), channel_id=1, source_target_pairs={{0,4},{4,0},{8,12},{12,8},{16,20},{20,16},{24,28},{28,24},{1,5},{5... | collective-permute-start | bytes 12582920 | tf_op jit(solution)/shard_map/ppermute | solution.py:80
  356.8 171.0 %all-gather.25.cloned.1.call-start = ((), (), s32[]{:S(2)}) async-start(), calls=%async_computation.7 | async-start | bytes 5242880 | tf_op jit(solution)/shard_map/all_gather | solution.py:107
  362.9 24.4 %copy-start.1 = (f32[4,512,1024]{2,1,0:T(8,128)}, f32[4,512,1024]{2,1,0:T(8,128)S(1)}, u32[]{:S(2)}) copy-start(f32[4,512,1024]{2,1,0:T(8,128)S(1)} %bitcast_add_fusion) | copy-start | bytes 25165828
  363.4 22.9 %collective-permute-start.18 = (bf16[2,256,1024]{2,1,0:T(8,128)(2,1)S(1)}, bf16[2,256,1024]{2,1,0:T(8,128)(2,1)S(1)}, u32[]{:S(2)}, u32[]{:S(2)}) collective-permute-start(bf16[2,256,1024]{2,1,0:T(8,128)(2,1)S(1)} %pad_maximum_fusion.7), channel_id=1, source_target_pairs={{0,16},{4,20},{8,24},{12,28},{16,0},{20,4},{24,8},{28,12},{1,17},{... | collective-permute-start | bytes 3145736 | tf_op jit(solution)/shard_map/ppermute | solution.py:93
  364.2 22.9 %collective-permute-start.16 = (bf16[2,256,1024]{2,1,0:T(8,128)(2,1)S(1)}, bf16[2,256,1024]{2,1,0:T(8,128)(2,1)S(1)}, u32[]{:S(2)}, u32[]{:S(2)}) collective-permute-start(bf16[2,256,1024]{2,1,0:T(8,128)(2,1)S(1)} %pad_maximum_fusion.6), channel_id=1, source_target_pairs={{0,8},{4,12},{8,0},{12,4},{16,24},{20,28},{24,16},{28,20},{1,9},{5... | collective-permute-start | bytes 3145736 | tf_op jit(solution)/shard_map/ppermute | solution.py:90
  388.7 11.8 %collective-permute-start.17 = (bf16[256,1024]{1,0:T(8,128)(2,1)}, bf16[256,1024]{1,0:T(8,128)(2,1)}, u32[]{:S(2)}, u32[]{:S(2)}) collective-permute-start(bf16[256,1024]{1,0:T(8,128)(2,1)} %get-tuple-element.17), channel_id=1, source_target_pairs={{0,16},{4,20},{8,24},{12,28},{16,0},{20,4},{24,8},{28,12},{1,17},{... | collective-permute-start | bytes 1572872 | tf_op jit(solution)/shard_map/ppermute | solution.py:100
  389.9 10.8 %collective-permute-start.19 = (bf16[256,1024]{1,0:T(8,128)(2,1)S(1)}, bf16[256,1024]{1,0:T(8,128)(2,1)}, u32[]{:S(2)}, u32[]{:S(2)}) collective-permute-start(bf16[256,1024]{1,0:T(8,128)(2,1)S(1)} %get-tuple-element.18), channel_id=1, source_target_pairs={{0,8},{4,12},{8,0},{12,4},{16,24},{20,28},{24,16},{28,20},{1,9},{5... | collective-permute-start | bytes 1572872 | tf_op jit(solution)/shard_map/ppermute | solution.py:103
  404.5 181.9 %all-gather.23.cloned.1.call-start = ((), (), s32[]{:S(2)}) async-start(), calls=%async_computation.6 | async-start | bytes 5242880 | tf_op jit(solution)/shard_map/all_gather | solution.py:107
  406.8 22.1 %collective-permute-start.13 = (bf16[2,64,4096]{2,1,0:T(8,128)(2,1)S(1)}, bf16[2,64,4096]{2,1,0:T(8,128)(2,1)S(1)}, u32[]{:S(2)}, u32[]{:S(2)}) collective-permute-start(bf16[2,64,4096]{2,1,0:T(8,128)(2,1)S(1)} %pad_maximum_fusion.4), channel_id=1, source_target_pairs={{0,16},{4,20},{8,24},{12,28},{16,0},{20,4},{24,8},{28,12},{1,17},{... | collective-permute-start | bytes 3145736 | tf_op jit(solution)/shard_map/ppermute | solution.py:93
  407.8 21.6 %collective-permute-start.11 = (bf16[2,64,4096]{2,1,0:T(8,128)(2,1)S(1)}, bf16[2,64,4096]{2,1,0:T(8,128)(2,1)S(1)}, u32[]{:S(2)}, u32[]{:S(2)}) collective-permute-start(bf16[2,64,4096]{2,1,0:T(8,128)(2,1)S(1)} %pad_maximum_fusion.3), channel_id=1, source_target_pairs={{0,8},{4,12},{8,0},{12,4},{16,24},{20,28},{24,16},{28,20},{1,9},{5... | collective-permute-start | bytes 3145736 | tf_op jit(solution)/shard_map/ppermute | solution.py:90
  431.6 9.6 %collective-permute-start.12 = (bf16[64,4096]{1,0:T(8,128)(2,1)S(1)}, bf16[64,4096]{1,0:T(8,128)(2,1)S(1)}, u32[]{:S(2)}, u32[]{:S(2)}) collective-permute-start(bf16[64,4096]{1,0:T(8,128)(2,1)S(1)} %get-tuple-element.23), channel_id=1, source_target_pairs={{0,16},{4,20},{8,24},{12,28},{16,0},{20,4},{24,8},{28,12},{1,17},{... | collective-permute-start | bytes 1572872 | tf_op jit(solution)/shard_map/ppermute | solution.py:100
  433.1 9.2 %collective-permute-start.14 = (bf16[64,4096]{1,0:T(8,128)(2,1)S(1)}, bf16[64,4096]{1,0:T(8,128)(2,1)S(1)}, u32[]{:S(2)}, u32[]{:S(2)}) collective-permute-start(bf16[64,4096]{1,0:T(8,128)(2,1)S(1)} %get-tuple-element.24), channel_id=1, source_target_pairs={{0,8},{4,12},{8,0},{12,4},{16,24},{20,28},{24,16},{28,20},{1,9},{5... | collective-permute-start | bytes 1572872 | tf_op jit(solution)/shard_map/ppermute | solution.py:103
  446.5 53.6 %copy-start.26 = (f32[512]{0:T(512)S(1)}, f32[512]{0:T(512)}, u32[]{:S(2)}) copy-start(f32[512]{0:T(512)} %copy-done.25) | copy-start | bytes 6148
  446.5 53.6 %copy-start.23 = (s32[512]{0:T(512)S(1)}, s32[512]{0:T(512)}, u32[]{:S(2)}) copy-start(s32[512]{0:T(512)} %param.14) | copy-start | bytes 6148
  (29 other events, 224.5 us)
Sparse Core Ops, SparseCore 0:
  9.9 48.1 all-gather.10
  59.9 27.7 all-gather.12
  89.6 54.2 all-gather.14
  145.6 54.2 all-gather.16
  330.8 27.9 all-gather.20
  360.7 62.8 all-gather.18
  425.1 80.3 all-gather.24
  507.1 79.2 all-gather.22
